TPU v7x, 32 devices: a whole 2x2x4 slice. The times are simulated.
32 devices in a mesh: row: 4 (over y, x), col: 8 (over z, core).
Axes of the slice: x: 2, y: 2, z: 4, core: 2. Of those that a mesh axis runs over, the one named last changes fastest.
Arguments:
- matrix_in: bfloat16 [2048, 2048], P('row', 'col'), as said below
- pattern: int32 [16, 16], replicated, may hold values from 0 to 1, as said below
Outputs:
- sign_step: float32 [2048, 2048], P('row', 'col')
Inputs may be any that keep to these rules, and one draw needn't show every extreme that they name: `pattern`: symmetric, every diagonal block is 1, and every block (i, (i + 8) mod 16) is 1. `matrix_in`: exactly symmetric.
All inputs are finite; a program needn't handle non-finite values.
Results may differ from a plain program's by a relative error of at most 0.0029.
Values may be sent and summed in bfloat16 or wider, within the bound.
No kernel may reach another device: no remote copies, remote signals or barrier semaphores. Data moves between devices by JAX's collectives and lax.ppermute only.
A program may use at most 64 MiB of HBM per device.

v0:
```python
import jax
import jax.numpy as jnp
from jax import lax
from jax.sharding import PartitionSpec as P

B = 128


def body(matrix_in, pattern):
    block_rows = matrix_in.shape[0] // B
    block_cols = matrix_in.shape[1] // B
    row_index = lax.axis_index("row")
    col_index = lax.axis_index("col")
    local_blocks = lax.dynamic_slice(
        pattern, (row_index * block_rows, col_index * block_cols), (block_rows, block_cols)
    )
    local_mask = jnp.repeat(jnp.repeat(local_blocks, B, axis=0), B, axis=1)
    masked = matrix_in * local_mask.astype(jnp.bfloat16)
    rows_all = lax.all_gather(masked, "col", axis=1, tiled=True)
    left_part = rows_all
    square = jnp.dot(
        left_part,
        lax.all_gather(masked, "row", axis=0, tiled=True),
        preferred_element_type=jnp.float32,
    )
    mask_float = local_mask.astype(jnp.float32)
    filtered = (mask_float * square).astype(jnp.bfloat16)
    left_part = rows_all
    cubic = jnp.dot(
        left_part,
        lax.all_gather(filtered, "row", axis=0, tiled=True),
        preferred_element_type=jnp.float32,
    )
    return mask_float * (1.5 * masked.astype(jnp.float32) - 0.5 * cubic)


def solution(mesh):
    return jax.shard_map(
        body, mesh=mesh, in_specs=(P("row", "col"), P()), out_specs=P("row", "col"), check_vma=False
    )
```

profile of v0, /device:TPU:0, one launch (start us, length us, event | category | flops | bytes accessed | tf_op | source)
XLA Modules:
  0.0 110.8 jit_solution(12114034085471506654)
XLA Ops:
  6.5 0.0 all-gather.6.cloned.1.call-start
  6.5 0.8 dynamic-slice_convert_fusion.1
  7.3 0.6 broadcast_in_dim.13
  7.9 1.7 %bitcast_multiply_fusion = bf16[512,256]{1,0:T(8,128)(2,1)} fusion(bf16[512,256]{1,0:T(8,128)(2,1)} %param.2, bf16[64,8,2,128]{3,2,1,0:T(2,128)(2,1)S(1)} %bitcast.13), kind=kLoop, calls=%fused_computation.5 | loop fusion | flops 131072 | bytes 786432 | tf_op jit(solution)/shard_map/mul | solution.py:18
  9.6 0.0 all-gather.6.cloned.1.call-update
  9.6 0.0 all-gather.4.cloned.1.call-start
  9.7 0.7 all-gather.4.cloned.1.call-update
  10.4 0.0 all-gather.8.cloned.1.call-start
  10.4 28.7 %all-gather.6.cloned.1.call-done = bf16[2048,256]{1,0:T(8,128)(2,1)} async-done(((bf16[512,256]{1,0:T(8,128)(2,1)}), bf16[2048,256]{1,0:T(8,128)(2,1)}) %all-gather.6.cloned.1.call-update) | async-done | bytes 1048592 | tf_op jit(solution)/shard_map/all_gather | solution.py:23
  39.1 32.5 %all-gather.4.cloned.1.call-done = bf16[512,2048]{1,0:T(8,128)(2,1)} async-done(((bf16[512,256]{1,0:T(8,128)(2,1)}), bf16[512,2048]{1,0:T(8,128)(2,1)}) %all-gather.4.cloned.1.call-update) | async-done | bytes 2097168 | tf_op jit(solution)/shard_map/all_gather | solution.py:19
  71.6 0.6 broadcast_in_dim.11
  72.2 0.0 copy-start
  72.2 0.0 copy-start.1
  72.2 3.4 %fusion.2 = bf16[512,256]{1,0:T(8,128)(2,1)} fusion(bf16[512,2048]{1,0:T(8,128)(2,1)} %all-gather.4.cloned.1.call-done, bf16[2048,256]{1,0:T(8,128)(2,1)} %all-gather.6.cloned.1.call-done, f32[64,8,2,128]{3,2,1,0:T(2,128)S(1)} %bitcast.16), kind=kOutput, calls=%fused_computation.4 | convolution fusion | flops 537133056 | bytes 3932160 | tf_op jit(solution)/shard_map/dot_general | solution.py:21
  75.7 0.0 all-gather.8.cloned.1.call-update
  75.7 25.9 %all-gather.8.cloned.1.call-done = bf16[2048,256]{1,0:T(8,128)(2,1)} async-done(((bf16[512,256]{1,0:T(8,128)(2,1)}), bf16[2048,256]{1,0:T(8,128)(2,1)}) %all-gather.8.cloned.1.call-update) | async-done | bytes 1048592 | tf_op jit(solution)/shard_map/all_gather | solution.py:31
  101.5 0.0 copy-done
  101.5 0.0 copy-done.1
  101.5 2.7 %fusion.1 = f32[512,256]{1,0:T(8,128)} fusion(bf16[512,2048]{1,0:T(8,128)(2,1)S(1)} %copy-done.1, bf16[2048,256]{1,0:T(8,128)(2,1)} %all-gather.8.cloned.1.call-done, bf16[512,256]{1,0:T(8,128)(2,1)S(1)} %copy-done, f32[64,8,2,128]{3,2,1,0:T(2,128)S(1)} %bitcast.17), kind=kOutput, calls=%fused_computation.3 | convolution fusion | flops 537526272 | bytes 4456448 | tf_op jit(solution)/shard_map/dot_general | solution.py:29
  (2 shorter events, 0.0 us)
Async XLA Ops:
  6.5 32.6 %all-gather.6.cloned.1.call-start = ((), (), s32[]{:S(2)}) async-start(), calls=%async_computation.1 | async-start | bytes 1310720 | tf_op jit(solution)/shard_map/all_gather | solution.py:23
  9.6 61.9 %all-gather.4.cloned.1.call-start = ((), (), s32[]{:S(2)}) async-start(), calls=%async_computation | async-start | bytes 2359296 | tf_op jit(solution)/shard_map/all_gather | solution.py:19
  10.4 91.1 %all-gather.8.cloned.1.call-start = ((), (), s32[]{:S(2)}) async-start(), calls=%async_computation.2 | async-start | bytes 1310720 | tf_op jit(solution)/shard_map/all_gather | solution.py:31
  72.2 29.3 %copy-start = (bf16[512,256]{1,0:T(8,128)(2,1)S(1)}, bf16[512,256]{1,0:T(8,128)(2,1)}, u32[]{:S(2)}) copy-start(bf16[512,256]{1,0:T(8,128)(2,1)} %bitcast_multiply_fusion) | copy-start | bytes 786436
  72.2 29.3 %copy-start.1 = (bf16[512,2048]{1,0:T(8,128)(2,1)S(1)}, bf16[512,2048]{1,0:T(8,128)(2,1)}, u32[]{:S(2)}) copy-start(bf16[512,2048]{1,0:T(8,128)(2,1)} %all-gather.4.cloned.1.call-done) | copy-start | bytes 6291460
Sparse Core Ops, SparseCore 0:
  9.8 29.3 all-gather.5
  40.7 30.8 all-gather.3
  75.8 25.6 all-gather.7
where the time goes:
time: 111 us
  waiting for transfers between devices  87.7 us (79%)
  between operations  13.1 us (12%)
  matrix products  6.16 us (6%)
  other arithmetic  2.45 us (2%)
  local copies, waits for them, and re-layouts  1.25 us (1%)
    all_gather x1, waiting for transfers between devices, body(): rows_all = lax.all_gather(masked, 'col', axis=1, tiled=True)  32.5 us
    all_gather x1, waiting for transfers between devices, body(): lax.all_gather(masked, 'row', axis=0, tiled=True)  28.7 us
    all_gather x1, waiting for transfers between devices, body(): lax.all_gather(filtered, 'row', axis=0, tiled=True)  25.9 us
    dot_general x1, matrix products, body(): jnp.dot(left_part, lax.all_gather(masked, 'row', axis=0, tiled=True), pre...  3.43 us
    dot_general x1, matrix products, body(): jnp.dot(left_part, lax.all_gather(filtered, 'row', axis=0, tiled=True), p...  2.73 us
  transfers between devices with their start and end apart: 3, of which 3 were waited for; matrix products, arithmetic and copies ran while one was open for 0% of the time, Pallas kernels for 0%

commit v1 on v0

--- a/solution.py
+++ b/solution.py
@@ -4,6 +4,17 @@
 from jax.sharding import PartitionSpec as P
 
 B = 128
+
+
+def gather_around(x, axis, dim):
+    ways = lax.axis_size(axis)
+    pieces = [x]
+    for far in range(1, ways):
+        pieces.append(
+            lax.ppermute(pieces[far - 1], axis, [(d, (d - 1) % ways) for d in range(ways)])
+        )
+    line = jnp.concatenate(pieces, axis=dim)
+    return jnp.roll(line, lax.axis_index(axis) * x.shape[dim], axis=dim)
 
 
 def body(matrix_in, pattern):
@@ -18,11 +29,7 @@
     masked = matrix_in * local_mask.astype(jnp.bfloat16)
     rows_all = lax.all_gather(masked, "col", axis=1, tiled=True)
     left_part = rows_all
-    square = jnp.dot(
-        left_part,
-        lax.all_gather(masked, "row", axis=0, tiled=True),
-        preferred_element_type=jnp.float32,
-    )
+    square = jnp.dot(left_part, gather_around(masked, "row", 0), preferred_element_type=jnp.float32)
     mask_float = local_mask.astype(jnp.float32)
     filtered = (mask_float * square).astype(jnp.bfloat16)
     left_part = rows_all

time: 111 us -> 83.4 us (0.75)
  waiting for transfers between devices: 87.7 us -> 47.8 us
  starting transfers between devices: 0.08 us -> 10.6 us
    all_gather x1 -> x0, waiting for transfers between devices: 28.7 us -> none  [body(): lax.all_gather(masked, 'row', axis=0, tiled=True)]
    all_gather x1, waiting for transfers between devices: 32.5 us -> 7.5 us  [body(): rows_all = lax.all_gather(masked, 'col', axis=1, tiled=True)]
    ppermute x0 -> x3, waiting for transfers between devices: none -> 14.4 us  [gather_around(): lax.ppermute(pieces[far - 1], axis, [(d, (d - 1) % ways) for d in range(w...]
    ppermute x0 -> x3, starting transfers between devices: none -> 10.6 us  [gather_around(): lax.ppermute(pieces[far - 1], axis, [(d, (d - 1) % ways) for d in range(w...]
    unnamed x0 -> x1, other arithmetic: none -> 1.73 us
    mul x1 -> x0, other arithmetic: 1.69 us -> none  [body(): masked = matrix_in * local_mask.astype(jnp.bfloat16)]
  transfers between devices with their start and end apart: 3 -> 5, of which waited for: 3 -> 5; matrix products, arithmetic and copies ran while one was open for 0% -> 1% of each run, Pallas kernels for 0% -> 0%
where the time goes in v1:
time: 83.4 us; the launch traced here: 83.2 us
  waiting for transfers between devices  47.8 us (57%)
  between operations  13.5 us (16%)
  starting transfers between devices  10.6 us (13%)
  matrix products  6.43 us (8%)
  other arithmetic  2.49 us (3%)
  local copies, waits for them, and re-layouts  2.33 us (3%)
    all_gather x1, waiting for transfers between devices, body(): lax.all_gather(filtered, 'row', axis=0, tiled=True)  25.9 us
    ppermute x3, waiting for transfers between devices, gather_around(): lax.ppermute(pieces[far - 1], axis, [(d, (d - 1) % ways) for d in range(w...  14.4 us
    ppermute x3, starting transfers between devices, gather_around(): lax.ppermute(pieces[far - 1], axis, [(d, (d - 1) % ways) for d in range(w...  10.6 us
    all_gather x1, waiting for transfers between devices, body(): rows_all = lax.all_gather(masked, 'col', axis=1, tiled=True)  7.5 us
    dot_general x1, matrix products, body(): jnp.dot(left_part, lax.all_gather(filtered, 'row', axis=0, tiled=True), p...  3.36 us
    dot_general x1, matrix products, body(): jnp.dot(left_part, gather_around(masked, 'row', 0), preferred_element_typ...  3.07 us
    unnamed x1, other arithmetic  1.73 us
  transfers between devices with their start and end apart: 5, of which 5 were waited for; matrix products, arithmetic and copies ran while one was open for 1% of the time, Pallas kernels for 0%

profile of v1, /device:TPU:0, one launch (start us, length us, event | category | flops | bytes accessed | tf_op | source)
XLA Modules:
  0.0 83.2 jit_solution(133203701422132999)
XLA Ops:
  6.5 0.0 all-gather.3.cloned.1.call-start
  6.5 0.8 dynamic-slice_convert_fusion.1
  7.3 0.6 broadcast_in_dim.13
  7.9 1.7 %constant_dynamic-update-slice_fusion.7 = (bf16[4096,256]{1,0:T(8,128)(2,1)S(1)}, bf16[512,256]{1,0:T(8,128)(2,1)}) fusion(bf16[512,256]{1,0:T(8,128)(2,1)} %param.2, bf16[64,8,2,128]{3,2,1,0:T(2,128)(2,1)S(1)} %bitcast.14), kind=kLoop, calls=%fused_computation.14 | loop fusion | flops 524287 | bytes 1048576
  9.7 0.0 all-gather.3.cloned.1.call-update
  9.7 0.0 all-gather.5.cloned.1.call-start
  9.7 3.9 %collective-permute-start = (bf16[512,256]{1,0:T(8,128)(2,1)}, bf16[512,256]{1,0:T(8,128)(2,1)S(1)}, u32[]{:S(2)}, u32[]{:S(2)}) collective-permute-start(bf16[512,256]{1,0:T(8,128)(2,1)} %get-tuple-element.6), channel_id=1, source_target_pairs={{0,24},{8,0},{16,8},{24,16},{1,25},{9,1},{17,9},{25,17},{2,26},{10... | collective-permute-start | bytes 786440 | tf_op jit(solution)/shard_map/ppermute | solution.py:14
  13.7 5.9 %collective-permute-done = bf16[512,256]{1,0:T(8,128)(2,1)S(1)} collective-permute-done((bf16[512,256]{1,0:T(8,128)(2,1)}, bf16[512,256]{1,0:T(8,128)(2,1)S(1)}, u32[]{:S(2)}, u32[]{:S(2)}) %collective-permute-start) | collective-permute-done | bytes 262176 | tf_op jit(solution)/shard_map/ppermute | solution.py:14
  19.6 3.3 %collective-permute-start.1 = (bf16[512,256]{1,0:T(8,128)(2,1)S(1)}, bf16[512,256]{1,0:T(8,128)(2,1)S(1)}, u32[]{:S(2)}, u32[]{:S(2)}) collective-permute-start(bf16[512,256]{1,0:T(8,128)(2,1)S(1)} %collective-permute-done), channel_id=1, source_target_pairs={{0,24},{8,0},{16,8},{24,16},{1,25},{9,1},{17,9},{25,17},{2,26},{10... | collective-permute-start | bytes 786440 | tf_op jit(solution)/shard_map/ppermute | solution.py:14
  22.8 4.7 %collective-permute-done.1 = bf16[512,256]{1,0:T(8,128)(2,1)S(1)} collective-permute-done((bf16[512,256]{1,0:T(8,128)(2,1)S(1)}, bf16[512,256]{1,0:T(8,128)(2,1)S(1)}, u32[]{:S(2)}, u32[]{:S(2)}) %collective-permute-start.1) | collective-permute-done | bytes 262176 | tf_op jit(solution)/shard_map/ppermute | solution.py:14
  27.5 3.4 %collective-permute-start.2 = (bf16[512,256]{1,0:T(8,128)(2,1)S(1)}, bf16[512,256]{1,0:T(8,128)(2,1)S(1)}, u32[]{:S(2)}, u32[]{:S(2)}) collective-permute-start(bf16[512,256]{1,0:T(8,128)(2,1)S(1)} %collective-permute-done.1), channel_id=1, source_target_pairs={{0,24},{8,0},{16,8},{24,16},{1,25},{9,1},{17,9},{25,17},{2,26},{10... | collective-permute-start | bytes 786440 | tf_op jit(solution)/shard_map/ppermute | solution.py:14
  31.0 3.8 %collective-permute-done.2 = bf16[512,256]{1,0:T(8,128)(2,1)S(1)} collective-permute-done((bf16[512,256]{1,0:T(8,128)(2,1)S(1)}, bf16[512,256]{1,0:T(8,128)(2,1)S(1)}, u32[]{:S(2)}, u32[]{:S(2)}) %collective-permute-start.2) | collective-permute-done | bytes 262176 | tf_op jit(solution)/shard_map/ppermute | solution.py:14
  34.8 1.0 %constant_dynamic-update-slice_fusion.3 = bf16[4096,256]{1,0:T(8,128)(2,1)S(1)} fusion(bf16[4096,256]{1,0:T(8,128)(2,1)S(1)} %constant_dynamic-update-slice_fusion.4, bf16[512,256]{1,0:T(8,128)(2,1)} %get-tuple-element.6), kind=kLoop, calls=%fused_computation.10 | loop fusion | bytes 524288
  35.9 7.5 %all-gather.3.cloned.1.call-done = bf16[512,2048]{1,0:T(8,128)(2,1)} async-done(((bf16[512,256]{1,0:T(8,128)(2,1)}), bf16[512,2048]{1,0:T(8,128)(2,1)}) %all-gather.3.cloned.1.call-update) | async-done | bytes 2097168 | tf_op jit(solution)/shard_map/all_gather | solution.py:30
  43.4 0.6 broadcast_in_dim.11
  44.0 0.0 copy-start
  44.0 3.1 %fusion.2 = bf16[512,256]{1,0:T(8,128)(2,1)} fusion(bf16[512,2048]{1,0:T(8,128)(2,1)} %all-gather.3.cloned.1.call-done, bf16[4096,256]{1,0:T(8,128)(2,1)S(1)} %constant_dynamic-update-slice_fusion, s32[]{:T(128)S(6)} %select_n.22, f32[64,8,2,128]{3,2,1,0:T(2,128)S(1)} %bitcast.16), kind=kOutput, calls=%fused_computation.4 | convolution fusion | flops 537133056 | bytes 3932164 | tf_op jit(solution)/shard_map/dot_general | solution.py:32
  47.1 0.0 all-gather.5.cloned.1.call-update
  47.1 25.9 %all-gather.5.cloned.1.call-done = bf16[2048,256]{1,0:T(8,128)(2,1)} async-done(((bf16[512,256]{1,0:T(8,128)(2,1)}), bf16[2048,256]{1,0:T(8,128)(2,1)}) %all-gather.5.cloned.1.call-update) | async-done | bytes 1048592 | tf_op jit(solution)/shard_map/all_gather | solution.py:38
  73.0 0.0 copy-done
  73.0 3.4 %fusion.1 = f32[512,256]{1,0:T(8,128)} fusion(bf16[512,2048]{1,0:T(8,128)(2,1)} %all-gather.3.cloned.1.call-done, bf16[2048,256]{1,0:T(8,128)(2,1)} %all-gather.5.cloned.1.call-done, bf16[512,256]{1,0:T(8,128)(2,1)S(1)} %copy-done, f32[64,8,2,128]{3,2,1,0:T(2,128)S(1)} %bitcast.17), kind=kOutput, calls=%fused_computation.3 | convolution fusion | flops 537526272 | bytes 4456448 | tf_op jit(solution)/shard_map/dot_general | solution.py:36
  (8 shorter events, 0.2 us)
Async XLA Ops:
  6.5 36.8 %all-gather.3.cloned.1.call-start = ((), (), s32[]{:S(2)}) async-start(), calls=%async_computation | async-start | bytes 2359296 | tf_op jit(solution)/shard_map/all_gather | solution.py:30
  9.7 63.3 %all-gather.5.cloned.1.call-start = ((), (), s32[]{:S(2)}) async-start(), calls=%async_computation.1 | async-start | bytes 1310720 | tf_op jit(solution)/shard_map/all_gather | solution.py:38
  9.7 9.8 %collective-permute-start = (bf16[512,256]{1,0:T(8,128)(2,1)}, bf16[512,256]{1,0:T(8,128)(2,1)S(1)}, u32[]{:S(2)}, u32[]{:S(2)}) collective-permute-start(bf16[512,256]{1,0:T(8,128)(2,1)} %get-tuple-element.6), channel_id=1, source_target_pairs={{0,24},{8,0},{16,8},{24,16},{1,25},{9,1},{17,9},{25,17},{2,26},{10... | collective-permute-start | bytes 786440 | tf_op jit(solution)/shard_map/ppermute | solution.py:14
  19.6 8.0 %collective-permute-start.1 = (bf16[512,256]{1,0:T(8,128)(2,1)S(1)}, bf16[512,256]{1,0:T(8,128)(2,1)S(1)}, u32[]{:S(2)}, u32[]{:S(2)}) collective-permute-start(bf16[512,256]{1,0:T(8,128)(2,1)S(1)} %collective-permute-done), channel_id=1, source_target_pairs={{0,24},{8,0},{16,8},{24,16},{1,25},{9,1},{17,9},{25,17},{2,26},{10... | collective-permute-start | bytes 786440 | tf_op jit(solution)/shard_map/ppermute | solution.py:14
  27.5 7.3 %collective-permute-start.2 = (bf16[512,256]{1,0:T(8,128)(2,1)S(1)}, bf16[512,256]{1,0:T(8,128)(2,1)S(1)}, u32[]{:S(2)}, u32[]{:S(2)}) collective-permute-start(bf16[512,256]{1,0:T(8,128)(2,1)S(1)} %collective-permute-done.1), channel_id=1, source_target_pairs={{0,24},{8,0},{16,8},{24,16},{1,25},{9,1},{17,9},{25,17},{2,26},{10... | collective-permute-start | bytes 786440 | tf_op jit(solution)/shard_map/ppermute | solution.py:14
  44.0 29.0 %copy-start = (bf16[512,256]{1,0:T(8,128)(2,1)S(1)}, bf16[512,256]{1,0:T(8,128)(2,1)}, u32[]{:S(2)}) copy-start(bf16[512,256]{1,0:T(8,128)(2,1)} %get-tuple-element.6) | copy-start | bytes 786436
Sparse Core Ops, SparseCore 0:
  9.8 33.5 all-gather.2
  47.2 25.6 all-gather.4
